TPU v7x, 32 devices: a whole 2x2x4 slice. The times are simulated.
32 devices in a mesh: blk: 16 (over z, y, core), rhs: 2 (over x).
Axes of the slice: x: 2, y: 2, z: 4, core: 2. Of those that a mesh axis runs over, the one named last changes fastest.
Arguments:
- factor_panel: float32 [2, 1024, 16384], P(None, None, 'blk'), may hold values from -0.0625 to 0.0625
- solved_before: float32 [16384, 512], P('blk', 'rhs'), may hold values from -6 to 6
- right_side: float32 [2, 1024, 512], P(None, None, 'rhs'), may hold values from -6 to 6
- diag_inverse: float32 [2, 1024, 1024], P(None, 'blk', 'rhs'), may hold values from -0.2 to 1.5, as said below
- coupling: float32 [1024, 1024], P(None, 'blk'), may hold values from -0.25 to 0.25
Outputs:
- solved: float32 [2, 1024, 512], P(None, 'blk', 'rhs')
Inputs may be any that keep to these rules, and one draw needn't show every extreme that they name: `diag_inverse`: each of the two blocks is lower triangular with a positive diagonal.
All inputs are finite; a program needn't handle non-finite values.
Results may differ from a plain program's by a relative error of at most 0.00009.
Values sent between devices are 32-bit elements; how exact they have to be, the bound alone decides.
No kernel may reach another device: no remote copies, remote signals or barrier semaphores. Data moves between devices by JAX's collectives and lax.ppermute only.
A program may use at most 64 MiB of HBM per device.

v0:
```python
import jax
import jax.numpy as jnp
from jax import lax
from jax.sharding import PartitionSpec as P


def product(left, right):
    return jnp.dot(left, right, precision=lax.Precision.HIGHEST, preferred_element_type=jnp.float32)


def shards(factor_panel, solved_before, right_side, diag_inverse, coupling):
    inverse_full = lax.all_gather(diag_inverse, "rhs", axis=2, tiled=True)
    own_count = diag_inverse.shape[1]
    my_index = lax.axis_index("blk")

    def own_slice(matrix):
        return lax.dynamic_slice_in_dim(matrix, my_index * own_count, own_count, 0)

    first_part = lax.psum_scatter(
        product(factor_panel[0], solved_before), "blk", scatter_dimension=0, tiled=True
    )
    first_remains = lax.all_gather(own_slice(right_side[0]) - first_part, "blk", axis=0, tiled=True)
    first_block = product(inverse_full[0], first_remains)
    panel_rows = factor_panel[1]
    second_part = lax.psum_scatter(
        product(panel_rows, solved_before) + product(coupling, first_block),
        "blk",
        scatter_dimension=0,
        tiled=True,
    )
    second_remains = lax.all_gather(
        own_slice(right_side[1]) - second_part, "blk", axis=0, tiled=True
    )
    second_block = product(inverse_full[1], second_remains)
    return jnp.stack([first_block, second_block])


def solution(mesh):
    placed = (
        P(None, None, "blk"),
        P("blk", "rhs"),
        P(None, None, "rhs"),
        P(None, "blk", "rhs"),
        P(None, "blk"),
    )
    return jax.shard_map(
        shards, mesh=mesh, in_specs=placed, out_specs=P(None, "blk", "rhs"), check_vma=False
    )
```

profile of v0, /device:TPU:0, one launch (start us, length us, event | category | flops | bytes accessed | tf_op | source)
XLA Modules:
  0.0 229.3 jit_solution(9284285652021798626)
XLA Ops:
  6.5 0.0 copy-start
  6.5 0.0 copy-start.1
  6.5 0.0 reduce-scatter.3.cloned.1.call-start
  6.5 1.2 copy-done
  7.8 6.6 %fusion.2 = f32[1024,256]{1,0:T(8,128)} fusion(f32[1024,256]{1,0:T(8,128)S(1)} %copy-done, f32[2,1024,1024]{2,1,0:T(8,128)} %param.5), kind=kOutput, calls=%fused_computation.2 | convolution fusion | flops 3221225472 | bytes 6291456 | tf_op jit(solution)/shard_map/dot_general | solution.py:8
  14.4 0.0 copy-start.2
  14.4 0.0 reduce-scatter.3.cloned.1.call-update
  14.4 0.0 all-gather.3.cloned.1.call-start
  14.5 0.0 copy-done.1
  14.5 1.5 fusion.10
  16.0 58.7 %reduce-scatter.3.cloned.1.call-done = f32[64,256]{1,0:T(8,128)} async-done(((f32[1024,256]{1,0:T(8,128)}), f32[64,256]{1,0:T(8,128)}) %reduce-scatter.3.cloned.1.call-update) | async-done | bytes 65552 | tf_op jit(solution)/shard_map/reduce_scatter | solution.py:19
  74.7 1.5 bitcast_subtract_fusion.1
  76.2 0.0 all-gather.3.cloned.1.call-update
  76.2 0.0 reduce-scatter.5.cloned.1.call-start
  76.3 0.0 copy-done.2
  76.3 7.0 %all_gather.10 = f32[2,64,1024]{2,1,0:T(8,128)S(1)} all-gather(f32[2,64,512]{2,1,0:T(8,128)S(1)} %copy-done.2), channel_id=1, replica_groups=mesh['blk'=16,'rhs'=2] {'rhs'}, dimensions={2}, use_global_device_ids=true | all-gather | bytes 786432 | tf_op jit(solution)/shard_map/all_gather | solution.py:12
  83.3 30.7 %all-gather.3.cloned.1.call-done = f32[1024,256]{1,0:T(8,128)} async-done(((f32[64,256]{1,0:T(8,128)}), f32[1024,256]{1,0:T(8,128)}) %all-gather.3.cloned.1.call-update) | async-done | bytes 1048592 | tf_op jit(solution)/shard_map/all_gather | solution.py:22
  114.0 2.0 fusion.9
  116.0 2.0 convolution_bitcast_fusion
  118.0 6.6 %fusion.6 = f32[1024,256]{1,0:T(8,128)} fusion(f32[1024,256]{1,0:T(8,128)S(1)} %convolution_bitcast_fusion, f32[1024,256]{1,0:T(8,128)S(1)} %copy-done, f32[2,1024,1024]{2,1,0:T(8,128)} %param.5), kind=kOutput, calls=%fused_computation.6 | convolution fusion | flops 3221487616 | bytes 7340032 | tf_op jit(solution)/shard_map/dot_general | solution.py:8
  124.6 0.0 reduce-scatter.5.cloned.1.call-update
  124.6 0.0 all-gather.5.cloned.1.call-start
  124.7 56.4 %reduce-scatter.5.cloned.1.call-done = f32[64,256]{1,0:T(8,128)} async-done(((f32[1024,256]{1,0:T(8,128)}), f32[64,256]{1,0:T(8,128)}) %reduce-scatter.5.cloned.1.call-update) | async-done | bytes 65552 | tf_op jit(solution)/shard_map/reduce_scatter | solution.py:25
  181.1 1.5 bitcast_subtract_fusion
  182.6 0.0 all-gather.5.cloned.1.call-update
  182.6 37.5 %all-gather.5.cloned.1.call-done = f32[1024,256]{1,0:T(8,128)} async-done(((f32[64,256]{1,0:T(8,128)}), f32[1024,256]{1,0:T(8,128)}) %all-gather.5.cloned.1.call-update) | async-done | bytes 1048592 | tf_op jit(solution)/shard_map/all_gather | solution.py:31
  220.1 2.0 convolution_bitcast_fusion.1
  222.1 0.7 pad_maximum_fusion
Async XLA Ops:
  6.5 1.2 copy-start
  6.5 7.9 %copy-start.1 = (f32[2,1024,256]{2,1,0:T(8,128)S(1)}, f32[2,1024,256]{2,1,0:T(8,128)}, u32[]{:S(2)}) copy-start(f32[2,1024,256]{2,1,0:T(8,128)} %param.7) | copy-start | bytes 6291460
  6.5 68.2 %reduce-scatter.3.cloned.1.call-start = ((), (), s32[]{:S(2)}) async-start(), calls=%async_computation.2 | async-start | bytes 1114112 | tf_op jit(solution)/shard_map/reduce_scatter | solution.py:19
  14.4 61.9 %copy-start.2 = (f32[2,64,512]{2,1,0:T(8,128)S(1)}, f32[2,64,512]{2,1,0:T(8,128)}, u32[]{:S(2)}) copy-start(f32[2,64,512]{2,1,0:T(8,128)} %param.8) | copy-start | bytes 786436
  14.4 99.6 %all-gather.3.cloned.1.call-start = ((), (), s32[]{:S(2)}) async-start(), calls=%async_computation.3 | async-start | bytes 1114112 | tf_op jit(solution)/shard_map/all_gather | solution.py:22
  76.2 104.9 %reduce-scatter.5.cloned.1.call-start = ((), (), s32[]{:S(2)}) async-start(), calls=%async_computation.4 | async-start | bytes 1114112 | tf_op jit(solution)/shard_map/reduce_scatter | solution.py:25
  124.6 95.5 %all-gather.5.cloned.1.call-start = ((), (), s32[]{:S(2)}) async-start(), calls=%async_computation.5 | async-start | bytes 1114112 | tf_op jit(solution)/shard_map/all_gather | solution.py:31
Sparse Core Ops, SparseCore 0:
  14.5 60.1 reduce-scatter.2
  77.1 36.8 all-gather.2
  124.7 56.3 reduce-scatter.4
  183.1 36.9 all-gather.4
where the time goes:
time: 230 us; the launch traced here: 229 us
  waiting for transfers between devices  183 us (80%)
  matrix products  19.1 us (8%)
  between operations  13.2 us (6%)
  blocking collectives  7.05 us (3%)
  other arithmetic  3.69 us (2%)
  local copies, waits for them, and re-layouts  2.72 us (1%)
    reduce_scatter x1, waiting for transfers between devices, shards(): lax.psum_scatter(product(factor_panel[0], solved_before), 'blk', scatter_...  58.7 us
    reduce_scatter x1, waiting for transfers between devices, shards(): lax.psum_scatter(product(panel_rows, solved_before) + product(coupling, f...  56.4 us
    all_gather x1, waiting for transfers between devices, shards(): lax.all_gather(own_slice(right_side[1]) - second_part, 'blk', axis=0, til...  37.5 us
    all_gather x1, waiting for transfers between devices, shards(): lax.all_gather(own_slice(right_side[0]) - first_part, 'blk', axis=0, tile...  30.7 us
    dot_general x5, matrix products, product(): jnp.dot(left, right, precision=lax.Precision.HIGHEST, preferred_element_t...  19.1 us
    all_gather x1, blocking collectives, shards(): inverse_full = lax.all_gather(diag_inverse, 'rhs', axis=2, tiled=True)  7.05 us
  transfers between devices with their start and end apart: 4, of which 4 were waited for; matrix products, arithmetic and copies ran while one was open for 1% of the time, Pallas kernels for 0%

commit v1 on v0

--- a/solution.py
+++ b/solution.py
@@ -2,6 +2,19 @@
 import jax.numpy as jnp
 from jax import lax
 from jax.sharding import PartitionSpec as P
+
+
+def ring_gather(value, axis, dim):
+    ways = lax.axis_size(axis)
+    up = [(d, (d + 1) % ways) for d in range(ways)]
+    down = [(d, (d - 1) % ways) for d in range(ways)]
+    earlier, later = ([value], [value])
+    for _ in range(ways // 2):
+        earlier.append(lax.ppermute(earlier[-1], axis, up))
+    for _ in range((ways - 1) // 2):
+        later.append(lax.ppermute(later[-1], axis, down))
+    line = jnp.concatenate([*earlier[::-1], *later[1:]], axis=dim)
+    return jnp.roll(line, (lax.axis_index(axis) - ways // 2) * value.shape[dim], axis=dim)
 
 
 def product(left, right):
@@ -28,9 +41,7 @@
         scatter_dimension=0,
         tiled=True,
     )
-    second_remains = lax.all_gather(
-        own_slice(right_side[1]) - second_part, "blk", axis=0, tiled=True
-    )
+    second_remains = ring_gather(own_slice(right_side[1]) - second_part, "blk", 0)
     second_block = product(inverse_full[1], second_remains)
     return jnp.stack([first_block, second_block])
 

time: 230 us -> 241 us (1.048)
  starting transfers between devices: 0.13 us -> 31.5 us
  waiting for transfers between devices: 183 us -> 166 us
    all_gather x1 -> x0, waiting for transfers between devices: 37.5 us -> none  [shards(): lax.all_gather(own_slice(right_side[1]) - second_part, 'blk', axis=0, til...]
    ppermute x0 -> x15, starting transfers between devices: none -> 31.4 us  [the longest x7 31.3 us: ring_gather(): later.append(lax.ppermute(later[-1], axis, down))]
    ppermute x0 -> x15, waiting for transfers between devices: none -> 19.9 us  [the longest x8 19.8 us: ring_gather(): earlier.append(lax.ppermute(earlier[-1], axis, up))]
  transfers between devices with their start and end apart: 4 -> 18, of which waited for: 4 -> 11; matrix products, arithmetic and copies ran while one was open for 1% -> 1% of each run, Pallas kernels for 0% -> 0%
where the time goes in v1:
time: 241 us
  waiting for transfers between devices  166 us (69%)
  starting transfers between devices  31.5 us (13%)
  matrix products  17 us (7%)
  between operations  13.4 us (6%)
  blocking collectives  7.05 us (3%)
  other arithmetic  3.06 us (1%)
  local copies, waits for them, and re-layouts  2.91 us (1%)
    reduce_scatter x1, waiting for transfers between devices, shards(): lax.psum_scatter(product(factor_panel[0], solved_before), 'blk', scatter_...  58.7 us
    reduce_scatter x1, waiting for transfers between devices, shards(): lax.psum_scatter(product(panel_rows, solved_before) + product(coupling, f...  56.5 us
    ppermute x7, starting transfers between devices, ring_gather(): later.append(lax.ppermute(later[-1], axis, down))  31.3 us
    all_gather x1, waiting for transfers between devices, shards(): lax.all_gather(own_slice(right_side[0]) - first_part, 'blk', axis=0, tile...  30.7 us
    ppermute x8, waiting for transfers between devices, ring_gather(): earlier.append(lax.ppermute(earlier[-1], axis, up))  19.8 us
    dot_general x5, matrix products, product(): jnp.dot(left, right, precision=lax.Precision.HIGHEST, preferred_element_t...  17 us
    all_gather x1, blocking collectives, shards(): inverse_full = lax.all_gather(diag_inverse, 'rhs', axis=2, tiled=True)  7.05 us
  transfers between devices with their start and end apart: 18, of which 11 were waited for; matrix products, arithmetic and copies ran while one was open for 1% of the time, Pallas kernels for 0%

profile of v1, /device:TPU:0, one launch (start us, length us, event | category | flops | bytes accessed | tf_op | source)
XLA Modules:
  0.0 240.8 jit_solution(12434817027093254538)
XLA Ops:
  6.5 0.0 copy-start
  6.5 0.0 reduce-scatter.3.cloned.1.call-start
  6.5 1.2 copy-done
  7.8 0.0 copy-start.1
  7.8 6.7 %fusion.2 = f32[1024,256]{1,0:T(8,128)} fusion(f32[1024,256]{1,0:T(8,128)S(1)} %copy-done, f32[2,1024,1024]{2,1,0:T(8,128)} %param.5), kind=kOutput, calls=%fused_computation.2 | convolution fusion | flops 3221225472 | bytes 6291456 | tf_op jit(solution)/shard_map/dot_general | solution.py:21
  14.5 0.0 reduce-scatter.3.cloned.1.call-update
  14.5 0.0 all-gather.2.cloned.1.call-start
  14.6 0.0 copy-done.1
  14.6 0.0 copy-start.2
  14.6 1.5 fusion.12
  16.0 0.0 copy-start.3
  16.0 58.7 %reduce-scatter.3.cloned.1.call-done = f32[64,256]{1,0:T(8,128)} async-done(((f32[1024,256]{1,0:T(8,128)}), f32[64,256]{1,0:T(8,128)}) %reduce-scatter.3.cloned.1.call-update) | async-done | bytes 65552 | tf_op jit(solution)/shard_map/reduce_scatter | solution.py:32
  74.8 1.5 bitcast_subtract_fusion.1
  76.3 0.0 all-gather.2.cloned.1.call-update
  76.3 0.0 reduce-scatter.5.cloned.1.call-start
  76.4 0.0 copy-done.2
  76.4 7.0 %all_gather.7 = f32[2,64,1024]{2,1,0:T(8,128)S(1)} all-gather(f32[2,64,512]{2,1,0:T(8,128)S(1)} %copy-done.2), channel_id=1, replica_groups=mesh['blk'=16,'rhs'=2] {'rhs'}, dimensions={2}, use_global_device_ids=true | all-gather | bytes 786432 | tf_op jit(solution)/shard_map/all_gather | solution.py:25
  83.4 30.7 %all-gather.2.cloned.1.call-done = f32[1024,256]{1,0:T(8,128)} async-done(((f32[64,256]{1,0:T(8,128)}), f32[1024,256]{1,0:T(8,128)}) %all-gather.2.cloned.1.call-update) | async-done | bytes 1048592 | tf_op jit(solution)/shard_map/all_gather | solution.py:35
  114.1 2.0 fusion.10
  116.1 0.0 copy-done.3
  116.1 1.0 convolution_bitcast_fusion
  117.1 6.6 %fusion.6 = f32[1024,256]{1,0:T(8,128)} fusion(f32[1024,256]{1,0:T(8,128)S(1)} %convolution_bitcast_fusion, f32[1024,256]{1,0:T(8,128)S(1)} %copy-done, f32[2,1024,1024]{2,1,0:T(8,128)} %param.5), kind=kOutput, calls=%fused_computation.6 | convolution fusion | flops 3221487616 | bytes 7340032 | tf_op jit(solution)/shard_map/dot_general | solution.py:21
  123.7 0.0 reduce-scatter.5.cloned.1.call-update
  123.7 56.5 %reduce-scatter.5.cloned.1.call-done = f32[64,256]{1,0:T(8,128)} async-done(((f32[1024,256]{1,0:T(8,128)}), f32[64,256]{1,0:T(8,128)}) %reduce-scatter.5.cloned.1.call-update) | async-done | bytes 65552 | tf_op jit(solution)/shard_map/reduce_scatter | solution.py:38
  180.2 0.9 bitcast_subtract_fusion
  181.1 0.1 collective-permute-start
  181.2 6.4 %collective-permute-done = f32[64,256]{1,0:T(8,128)S(1)} collective-permute-done((f32[64,256]{1,0:T(8,128)S(1)}, f32[64,256]{1,0:T(8,128)S(1)}, u32[]{:S(2)}, u32[]{:S(2)}) %collective-permute-start) | collective-permute-done | bytes 65568 | tf_op jit(solution)/shard_map/ppermute | solution.py:13
  187.6 0.0 collective-permute-start.1
  187.6 4.4 %collective-permute-start.8 = (f32[64,256]{1,0:T(8,128)S(1)}, f32[64,256]{1,0:T(8,128)S(1)}, u32[]{:S(2)}, u32[]{:S(2)}) collective-permute-start(f32[64,256]{1,0:T(8,128)S(1)} %bitcast_subtract_fusion), channel_id=1, source_target_pairs={{0,30},{2,0},{4,2},{6,4},{8,6},{10,8},{12,10},{14,12},{16,14},{18,... | collective-permute-start | bytes 196616 | tf_op jit(solution)/shard_map/ppermute | solution.py:15
  192.0 2.0 collective-permute-done.1
  194.1 0.0 collective-permute-start.2
  194.1 0.0 collective-permute-done.8
  194.1 4.4 %collective-permute-start.9 = (f32[64,256]{1,0:T(8,128)S(1)}, f32[64,256]{1,0:T(8,128)S(1)}, u32[]{:S(2)}, u32[]{:S(2)}) collective-permute-start(f32[64,256]{1,0:T(8,128)S(1)} %collective-permute-done.8), channel_id=1, source_target_pairs={{0,30},{2,0},{4,2},{6,4},{8,6},{10,8},{12,10},{14,12},{16,14},{18,... | collective-permute-start | bytes 196616 | tf_op jit(solution)/shard_map/ppermute | solution.py:15
  198.5 1.9 collective-permute-done.2
  200.4 0.0 collective-permute-start.3
  200.4 0.0 collective-permute-done.9
  200.4 4.5 %collective-permute-start.10 = (f32[64,256]{1,0:T(8,128)S(1)}, f32[64,256]{1,0:T(8,128)S(1)}, u32[]{:S(2)}, u32[]{:S(2)}) collective-permute-start(f32[64,256]{1,0:T(8,128)S(1)} %collective-permute-done.9), channel_id=1, source_target_pairs={{0,30},{2,0},{4,2},{6,4},{8,6},{10,8},{12,10},{14,12},{16,14},{18,... | collective-permute-start | bytes 196616 | tf_op jit(solution)/shard_map/ppermute | solution.py:15
  204.9 1.9 collective-permute-done.3
  206.8 0.0 collective-permute-start.4
  206.8 0.0 collective-permute-done.10
  206.9 4.5 %collective-permute-start.11 = (f32[64,256]{1,0:T(8,128)S(1)}, f32[64,256]{1,0:T(8,128)S(1)}, u32[]{:S(2)}, u32[]{:S(2)}) collective-permute-start(f32[64,256]{1,0:T(8,128)S(1)} %collective-permute-done.10), channel_id=1, source_target_pairs={{0,30},{2,0},{4,2},{6,4},{8,6},{10,8},{12,10},{14,12},{16,14},{18,... | collective-permute-start | bytes 196616 | tf_op jit(solution)/shard_map/ppermute | solution.py:15
  211.3 1.9 collective-permute-done.4
  213.2 0.0 collective-permute-start.5
  213.2 0.0 collective-permute-done.11
  213.2 4.5 %collective-permute-start.12 = (f32[64,256]{1,0:T(8,128)S(1)}, f32[64,256]{1,0:T(8,128)S(1)}, u32[]{:S(2)}, u32[]{:S(2)}) collective-permute-start(f32[64,256]{1,0:T(8,128)S(1)} %collective-permute-done.11), channel_id=1, source_target_pairs={{0,30},{2,0},{4,2},{6,4},{8,6},{10,8},{12,10},{14,12},{16,14},{18,... | collective-permute-start | bytes 196616 | tf_op jit(solution)/shard_map/ppermute | solution.py:15
  217.7 1.9 collective-permute-done.5
  219.6 0.0 collective-permute-start.6
  219.6 0.0 collective-permute-done.12
  219.6 4.5 %collective-permute-start.13 = (f32[64,256]{1,0:T(8,128)S(1)}, f32[64,256]{1,0:T(8,128)S(1)}, u32[]{:S(2)}, u32[]{:S(2)}) collective-permute-start(f32[64,256]{1,0:T(8,128)S(1)} %collective-permute-done.12), channel_id=1, source_target_pairs={{0,30},{2,0},{4,2},{6,4},{8,6},{10,8},{12,10},{14,12},{16,14},{18,... | collective-permute-start | bytes 196616 | tf_op jit(solution)/shard_map/ppermute | solution.py:15
  224.1 1.9 collective-permute-done.6
  226.0 0.0 collective-permute-start.7
  226.0 0.0 collective-permute-done.13
  226.0 4.5 %collective-permute-start.14 = (f32[64,256]{1,0:T(8,128)S(1)}, f32[64,256]{1,0:T(8,128)S(1)}, u32[]{:S(2)}, u32[]{:S(2)}) collective-permute-start(f32[64,256]{1,0:T(8,128)S(1)} %collective-permute-done.13), channel_id=1, source_target_pairs={{0,30},{2,0},{4,2},{6,4},{8,6},{10,8},{12,10},{14,12},{16,14},{18,... | collective-permute-start | bytes 196616 | tf_op jit(solution)/shard_map/ppermute | solution.py:15
  230.5 1.9 collective-permute-done.7
  232.6 0.0 collective-permute-done.14
  232.9 0.8 convolution_bitcast_fusion.1
  233.6 0.7 pad_maximum_fusion
  (32 shorter events, 0.2 us)
Async XLA Ops:
  6.5 1.2 copy-start
  6.5 68.2 %reduce-scatter.3.cloned.1.call-start = ((), (), s32[]{:S(2)}) async-start(), calls=%async_computation.2 | async-start | bytes 1114112 | tf_op jit(solution)/shard_map/reduce_scatter | solution.py:32
  7.8 6.8 %copy-start.1 = (f32[2,1024,256]{2,1,0:T(8,128)S(1)}, f32[2,1024,256]{2,1,0:T(8,128)}, u32[]{:S(2)}) copy-start(f32[2,1024,256]{2,1,0:T(8,128)} %param.7) | copy-start | bytes 6291460
  14.5 99.6 %all-gather.2.cloned.1.call-start = ((), (), s32[]{:S(2)}) async-start(), calls=%async_computation.3 | async-start | bytes 1114112 | tf_op jit(solution)/shard_map/all_gather | solution.py:35
  14.6 61.8 %copy-start.2 = (f32[2,64,512]{2,1,0:T(8,128)S(1)}, f32[2,64,512]{2,1,0:T(8,128)}, u32[]{:S(2)}) copy-start(f32[2,64,512]{2,1,0:T(8,128)} %param.8) | copy-start | bytes 786436
  16.0 100.0 %copy-start.3 = (f32[1024,64]{0,1:T(8,128)S(1)}, f32[1024,64]{0,1:T(8,128)}, u32[]{:S(2)}) copy-start(f32[1024,64]{0,1:T(8,128)} %param.9) | copy-start | bytes 786436
  76.3 103.9 %reduce-scatter.5.cloned.1.call-start = ((), (), s32[]{:S(2)}) async-start(), calls=%async_computation.4 | async-start | bytes 1114112 | tf_op jit(solution)/shard_map/reduce_scatter | solution.py:38
  181.1 6.4 %collective-permute-start = (f32[64,256]{1,0:T(8,128)S(1)}, f32[64,256]{1,0:T(8,128)S(1)}, u32[]{:S(2)}, u32[]{:S(2)}) collective-permute-start(f32[64,256]{1,0:T(8,128)S(1)} %bitcast_subtract_fusion), channel_id=1, source_target_pairs={{0,2},{2,4},{4,6},{6,8},{8,10},{10,12},{12,14},{14,16},{16,18},{18... | collective-permute-start | bytes 196616 | tf_op jit(solution)/shard_map/ppermute | solution.py:13
  187.6 6.5 %collective-permute-start.1 = (f32[64,256]{1,0:T(8,128)S(1)}, f32[64,256]{1,0:T(8,128)S(1)}, u32[]{:S(2)}, u32[]{:S(2)}) collective-permute-start(f32[64,256]{1,0:T(8,128)S(1)} %collective-permute-done), channel_id=1, source_target_pairs={{0,2},{2,4},{4,6},{6,8},{8,10},{10,12},{12,14},{14,16},{16,18},{18... | collective-permute-start | bytes 196616 | tf_op jit(solution)/shard_map/ppermute | solution.py:13
  187.6 6.5 %collective-permute-start.8 = (f32[64,256]{1,0:T(8,128)S(1)}, f32[64,256]{1,0:T(8,128)S(1)}, u32[]{:S(2)}, u32[]{:S(2)}) collective-permute-start(f32[64,256]{1,0:T(8,128)S(1)} %bitcast_subtract_fusion), channel_id=1, source_target_pairs={{0,30},{2,0},{4,2},{6,4},{8,6},{10,8},{12,10},{14,12},{16,14},{18,... | collective-permute-start | bytes 196616 | tf_op jit(solution)/shard_map/ppermute | solution.py:15
  194.1 6.4 %collective-permute-start.2 = (f32[64,256]{1,0:T(8,128)S(1)}, f32[64,256]{1,0:T(8,128)S(1)}, u32[]{:S(2)}, u32[]{:S(2)}) collective-permute-start(f32[64,256]{1,0:T(8,128)S(1)} %collective-permute-done.1), channel_id=1, source_target_pairs={{0,2},{2,4},{4,6},{6,8},{8,10},{10,12},{12,14},{14,16},{16,18},{18... | collective-permute-start | bytes 196616 | tf_op jit(solution)/shard_map/ppermute | solution.py:13
  194.1 6.4 %collective-permute-start.9 = (f32[64,256]{1,0:T(8,128)S(1)}, f32[64,256]{1,0:T(8,128)S(1)}, u32[]{:S(2)}, u32[]{:S(2)}) collective-permute-start(f32[64,256]{1,0:T(8,128)S(1)} %collective-permute-done.8), channel_id=1, source_target_pairs={{0,30},{2,0},{4,2},{6,4},{8,6},{10,8},{12,10},{14,12},{16,14},{18,... | collective-permute-start | bytes 196616 | tf_op jit(solution)/shard_map/ppermute | solution.py:15
  200.4 6.4 %collective-permute-start.3 = (f32[64,256]{1,0:T(8,128)S(1)}, f32[64,256]{1,0:T(8,128)S(1)}, u32[]{:S(2)}, u32[]{:S(2)}) collective-permute-start(f32[64,256]{1,0:T(8,128)S(1)} %collective-permute-done.2), channel_id=1, source_target_pairs={{0,2},{2,4},{4,6},{6,8},{8,10},{10,12},{12,14},{14,16},{16,18},{18... | collective-permute-start | bytes 196616 | tf_op jit(solution)/shard_map/ppermute | solution.py:13
  200.4 6.4 %collective-permute-start.10 = (f32[64,256]{1,0:T(8,128)S(1)}, f32[64,256]{1,0:T(8,128)S(1)}, u32[]{:S(2)}, u32[]{:S(2)}) collective-permute-start(f32[64,256]{1,0:T(8,128)S(1)} %collective-permute-done.9), channel_id=1, source_target_pairs={{0,30},{2,0},{4,2},{6,4},{8,6},{10,8},{12,10},{14,12},{16,14},{18,... | collective-permute-start | bytes 196616 | tf_op jit(solution)/shard_map/ppermute | solution.py:15
  206.8 6.4 %collective-permute-start.4 = (f32[64,256]{1,0:T(8,128)S(1)}, f32[64,256]{1,0:T(8,128)S(1)}, u32[]{:S(2)}, u32[]{:S(2)}) collective-permute-start(f32[64,256]{1,0:T(8,128)S(1)} %collective-permute-done.3), channel_id=1, source_target_pairs={{0,2},{2,4},{4,6},{6,8},{8,10},{10,12},{12,14},{14,16},{16,18},{18... | collective-permute-start | bytes 196616 | tf_op jit(solution)/shard_map/ppermute | solution.py:13
  206.9 6.4 %collective-permute-start.11 = (f32[64,256]{1,0:T(8,128)S(1)}, f32[64,256]{1,0:T(8,128)S(1)}, u32[]{:S(2)}, u32[]{:S(2)}) collective-permute-start(f32[64,256]{1,0:T(8,128)S(1)} %collective-permute-done.10), channel_id=1, source_target_pairs={{0,30},{2,0},{4,2},{6,4},{8,6},{10,8},{12,10},{14,12},{16,14},{18,... | collective-permute-start | bytes 196616 | tf_op jit(solution)/shard_map/ppermute | solution.py:15
  213.2 6.4 %collective-permute-start.5 = (f32[64,256]{1,0:T(8,128)S(1)}, f32[64,256]{1,0:T(8,128)S(1)}, u32[]{:S(2)}, u32[]{:S(2)}) collective-permute-start(f32[64,256]{1,0:T(8,128)S(1)} %collective-permute-done.4), channel_id=1, source_target_pairs={{0,2},{2,4},{4,6},{6,8},{8,10},{10,12},{12,14},{14,16},{16,18},{18... | collective-permute-start | bytes 196616 | tf_op jit(solution)/shard_map/ppermute | solution.py:13
  213.2 6.4 %collective-permute-start.12 = (f32[64,256]{1,0:T(8,128)S(1)}, f32[64,256]{1,0:T(8,128)S(1)}, u32[]{:S(2)}, u32[]{:S(2)}) collective-permute-start(f32[64,256]{1,0:T(8,128)S(1)} %collective-permute-done.11), channel_id=1, source_target_pairs={{0,30},{2,0},{4,2},{6,4},{8,6},{10,8},{12,10},{14,12},{16,14},{18,... | collective-permute-start | bytes 196616 | tf_op jit(solution)/shard_map/ppermute | solution.py:15
  219.6 6.4 %collective-permute-start.6 = (f32[64,256]{1,0:T(8,128)S(1)}, f32[64,256]{1,0:T(8,128)S(1)}, u32[]{:S(2)}, u32[]{:S(2)}) collective-permute-start(f32[64,256]{1,0:T(8,128)S(1)} %collective-permute-done.5), channel_id=1, source_target_pairs={{0,2},{2,4},{4,6},{6,8},{8,10},{10,12},{12,14},{14,16},{16,18},{18... | collective-permute-start | bytes 196616 | tf_op jit(solution)/shard_map/ppermute | solution.py:13
  219.6 6.4 %collective-permute-start.13 = (f32[64,256]{1,0:T(8,128)S(1)}, f32[64,256]{1,0:T(8,128)S(1)}, u32[]{:S(2)}, u32[]{:S(2)}) collective-permute-start(f32[64,256]{1,0:T(8,128)S(1)} %collective-permute-done.12), channel_id=1, source_target_pairs={{0,30},{2,0},{4,2},{6,4},{8,6},{10,8},{12,10},{14,12},{16,14},{18,... | collective-permute-start | bytes 196616 | tf_op jit(solution)/shard_map/ppermute | solution.py:15
  226.0 6.4 %collective-permute-start.7 = (f32[64,256]{1,0:T(8,128)S(1)}, f32[64,256]{1,0:T(8,128)S(1)}, u32[]{:S(2)}, u32[]{:S(2)}) collective-permute-start(f32[64,256]{1,0:T(8,128)S(1)} %collective-permute-done.6), channel_id=1, source_target_pairs={{0,2},{2,4},{4,6},{6,8},{8,10},{10,12},{12,14},{14,16},{16,18},{18... | collective-permute-start | bytes 196616 | tf_op jit(solution)/shard_map/ppermute | solution.py:13
  226.0 6.6 %collective-permute-start.14 = (f32[64,256]{1,0:T(8,128)S(1)}, f32[64,256]{1,0:T(8,128)S(1)}, u32[]{:S(2)}, u32[]{:S(2)}) collective-permute-start(f32[64,256]{1,0:T(8,128)S(1)} %collective-permute-done.13), channel_id=1, source_target_pairs={{0,30},{2,0},{4,2},{6,4},{8,6},{10,8},{12,10},{14,12},{16,14},{18,... | collective-permute-start | bytes 196616 | tf_op jit(solution)/shard_map/ppermute | solution.py:15
Sparse Core Ops, SparseCore 0:
  14.6 60.1 reduce-scatter.2
  77.2 36.8 all-gather.1
  123.8 56.3 reduce-scatter.4
